TPU v7x, 128 devices: a whole 4x4x4 slice. The times are simulated.
128 devices in a mesh: dp: 8 (over z, core), ts: 16 (over y, x).
Axes of the slice: x: 4, y: 4, z: 4, core: 2. Of those that a mesh axis runs over, the one named last changes fastest.
Arguments:
- text_embed: bfloat16 [8, 1024, 4096], P('dp', None, 'ts'), may hold values from -6 to 6
- bridge: bfloat16 [128, 32, 4096], P('dp', None, 'ts'), may hold values from -6 to 6
- crystal_slot: int32 [128], P('dp'), may hold values from 0 to 8159, as said below
- segments: int32 [8, 1024], P('dp'), may hold values from 0 to 15, as said below
- attn_gain: float32 [4096], replicated, may hold values from 0.1 to 1.9
- w_query: bfloat16 [4096, 4096], P(None, 'ts'), as said below
- w_key: bfloat16 [4096, 1024], P(None, 'ts'), may hold values from -0.09375 to 0.09375
- w_value: bfloat16 [4096, 1024], P(None, 'ts'), may hold values from -0.09375 to 0.09375
- w_out: bfloat16 [4096, 4096], P('ts'), may hold values from -0.09375 to 0.09375
- mlp_gain: float32 [4096], replicated, may hold values from 0.1 to 1.9
- w_gate: bfloat16 [4096, 12288], P(None, 'ts'), may hold values from -0.09375 to 0.09375
- w_up: bfloat16 [4096, 12288], P(None, 'ts'), may hold values from -0.09375 to 0.09375
- w_down: bfloat16 [12288, 4096], P('ts'), may hold values from -0.0546875 to 0.0546875
Outputs:
- layer_out: bfloat16 [8, 1024, 4096], P('dp', 'ts')
Inputs may be any that keep to these rules, and one draw needn't show every extreme that they name: `segments`: each row starts at 0, never falls and names every document number of 0 to 15; every document holds at least 33 positions. `crystal_slot`: each crystal's 32 rows take the first 32 positions of one document, given as sequence * 1024 + that document's first position; every document takes exactly one crystal, and each sequence takes exactly 2 of the 16 crystals held by each index of dp. `w_query`: entries lie within plus or minus 104 / sqrt(4096).
All inputs are finite; a program needn't handle non-finite values.
Results may differ from a plain program's by a relative error of at most 0.025.
The roundings to bfloat16 on the way count: a program that leaves them out, or rounds other values in their place, can miss the bound.
Values may be sent and summed in bfloat16 or wider, within the bound.
No kernel may reach another device: no remote copies, remote signals or barrier semaphores. Data moves between devices by JAX's collectives and lax.ppermute only.
A program may use at most 128 MiB of HBM per device.

v0:
```python
import jax
import jax.numpy as jnp
from jax import lax
from jax.sharding import PartitionSpec as P

HD = 128
DOC_LEN = 64
ROW_CHUNKS = 2
COL_CHUNKS = 2
norm_epsilon = 1e-05
rope_base = 500000.0
masked_score = -1e30


def partner_2(block, axis, apart):
    count = lax.axis_size(axis)
    route = []
    for low in range(count):
        high = low | 1 << apart
        if high != low and high < count:
            route += [(low, high), (high, low)]
    return lax.ppermute(block, axis, route)


def norm_rows(rows, gain):
    widened = rows.astype(jnp.float32)
    inverse_rms = lax.rsqrt(jnp.mean(widened * widened, axis=-1, keepdims=True) + norm_epsilon)
    return (widened * inverse_rms * gain).astype(jnp.bfloat16)


def rotate_pairs(values, positions, first_pair):
    pair_count = values.shape[-1] // 2
    exponent = 2.0 * (first_pair + jnp.arange(pair_count, dtype=jnp.int32)).astype(jnp.float32) / HD
    frequency = rope_base ** (-exponent)
    angles = positions.astype(jnp.float32)[:, None] * frequency[None, :]
    cosine = jnp.cos(angles)[:, None, :]
    sine_part = jnp.sin(angles)[:, None, :]
    paired = values.reshape(values.shape[0], values.shape[1], pair_count, 2)
    even_part = paired[..., 0]
    odd_part = paired[..., 1]
    new_even = even_part * cosine - odd_part * sine_part
    new_odd = even_part * sine_part + odd_part * cosine
    return jnp.stack([new_even, new_odd], axis=-1).reshape(values.shape)


def attend_block(query_block, query_segments, query_index, keys_full, values_full, segment_ids):
    scores = jnp.einsum(
        "qhd,kd->hqk", query_block, keys_full, preferred_element_type=jnp.float32
    ) * HD ** (-0.5)
    key_index = jnp.arange(keys_full.shape[0], dtype=jnp.int32)
    allowed = (query_segments[:, None] == segment_ids[None, :]) & (
        key_index[None, :] <= query_index[:, None]
    )
    scores = jnp.where(allowed[None], scores, masked_score)
    row_top = jnp.max(scores, axis=-1, keepdims=True)
    weights = jnp.exp(scores - row_top)
    probabilities = (weights / jnp.sum(weights, axis=-1, keepdims=True)).astype(jnp.bfloat16)
    mixed_rows = jnp.einsum(
        "hqk,kd->qhd", probabilities, values_full, preferred_element_type=jnp.float32
    )
    return mixed_rows.astype(jnp.bfloat16).reshape(query_block.shape[0], -1)


def after(ready, value):
    return lax.optimization_barrier((ready, value))[1]


def shards(
    text_embed,
    bridge,
    crystal_slot,
    segments,
    attn_gain,
    w_query,
    w_key,
    w_value,
    w_out,
    mlp_gain,
    w_gate,
    w_up,
    w_down,
):
    seq_len = text_embed.shape[1]
    part_width = text_embed.shape[2]
    doc_count = seq_len // DOC_LEN
    bridge_len = bridge.shape[1]
    tok_rows = seq_len // lax.axis_size("ts")
    group_index = lax.axis_index("dp")
    ts_index = lax.axis_index("ts")
    segment_ids = segments[0]
    doc_numbers = jnp.arange(doc_count, dtype=jnp.int32)
    starts = jnp.sum((segment_ids[None, :] < doc_numbers[:, None]).astype(jnp.int32), axis=1)
    doc_match = segment_ids[:, None] == doc_numbers[None, :]
    positions = jnp.arange(seq_len, dtype=jnp.int32) - jnp.sum(
        jnp.where(doc_match, starts[None, :], 0), axis=1
    )
    flat_bridge = bridge.reshape(bridge.shape[0], bridge_len * part_width)
    slot_high = (crystal_slot // 128).astype(jnp.bfloat16)
    slot_low = (crystal_slot % 128).astype(jnp.bfloat16)
    slot_cols = jnp.zeros((bridge.shape[0], 128), jnp.bfloat16)
    slot_cols = slot_cols.at[:, 0].set(slot_high).at[:, 1].set(slot_low)
    arrived_all = lax.all_gather(
        jnp.concatenate([flat_bridge, slot_cols], axis=1), "dp", axis=0, tiled=True
    )
    arrived = arrived_all[:, : bridge_len * part_width]
    arrived_slots = arrived_all[:, -128].astype(jnp.int32) * 128 + arrived_all[:, -127].astype(
        jnp.int32
    )
    wanted = group_index * seq_len + starts
    picking = wanted[:, None] == arrived_slots[None, :]
    by_doc = jnp.dot(
        picking.astype(jnp.bfloat16), arrived, preferred_element_type=jnp.float32
    ).astype(jnp.bfloat16)
    by_doc = by_doc.reshape(doc_count * bridge_len, part_width)
    in_bridge = positions < bridge_len
    row_pick = (segment_ids * bridge_len + positions)[:, None] == jnp.arange(
        doc_count * bridge_len, dtype=jnp.int32
    )[None, :]
    row_pick = row_pick & in_bridge[:, None]
    filled = jnp.dot(
        row_pick.astype(jnp.bfloat16), by_doc, preferred_element_type=jnp.float32
    ).astype(jnp.bfloat16)
    own_part = jnp.where(in_bridge[:, None], filled, text_embed[0])
    chunk_rows = seq_len // ROW_CHUNKS
    heads_here = w_query.shape[1] // HD
    kv_cols = w_key.shape[1]
    upper_half = ts_index % 2 == 1
    packed_chunks = []
    keys_chunks = []
    values_chunks = []
    after_chunks = []
    hidden_chunks = []
    previous = None
    previous_sum = None
    gate = None
    for chunk in range(ROW_CHUNKS):
        rows = slice(chunk * chunk_rows, (chunk + 1) * chunk_rows)
        local_rows = own_part[rows]
        if previous is not None:
            local_rows = after(previous, local_rows)
        packed = lax.all_gather(local_rows, "ts", axis=1, tiled=True)
        previous = packed
        if gate is not None:
            packed = after(gate, packed)
        packed_chunks.append(packed)
        chunk_positions = positions[rows]
        normed = norm_rows(packed, attn_gain)
        queries = jnp.dot(normed, w_query, preferred_element_type=jnp.float32).reshape(
            chunk_rows, heads_here, HD
        )
        queries = rotate_pairs(queries, chunk_positions, 0).astype(jnp.bfloat16)
        key_half = jnp.dot(normed, w_key, preferred_element_type=jnp.float32).reshape(
            chunk_rows, 1, kv_cols
        )
        key_half = rotate_pairs(key_half, chunk_positions, ts_index % 2 * (kv_cols // 2))
        key_half = key_half.astype(jnp.bfloat16).reshape(chunk_rows, kv_cols)
        value_half = jnp.dot(normed, w_value, preferred_element_type=jnp.float32).astype(
            jnp.bfloat16
        )
        own_pair = jnp.concatenate([key_half, value_half], axis=1)
        partner = partner_2(own_pair, "ts", 0)
        lower_half = jnp.where(upper_half, partner, own_pair)
        higher = jnp.where(upper_half, own_pair, partner)
        keys_chunks.append(jnp.concatenate([lower_half[:, :kv_cols], higher[:, :kv_cols]], axis=1))
        values_chunks.append(
            jnp.concatenate([lower_half[:, kv_cols:], higher[:, kv_cols:]], axis=1)
        )
        keys_seen = jnp.concatenate(keys_chunks, axis=0)
        values_seen = jnp.concatenate(values_chunks, axis=0)
        end_row = (chunk + 1) * chunk_rows
        query_index = jnp.arange(chunk * chunk_rows, end_row, dtype=jnp.int32)
        attended = attend_block(
            queries, segment_ids[rows], query_index, keys_seen, values_seen, segment_ids[:end_row]
        )
        gate = attended
        partial_rows = jnp.dot(attended, w_out, preferred_element_type=jnp.float32).astype(
            jnp.bfloat16
        )
        if previous_sum is not None:
            partial_rows = after(previous_sum, partial_rows)
        attn_sum = lax.psum(partial_rows, "ts")
        previous_sum = attn_sum
        after_attn = (packed.astype(jnp.float32) + attn_sum.astype(jnp.float32)).astype(
            jnp.bfloat16
        )
        after_chunks.append(after_attn)
        normed_mlp = norm_rows(after_attn, mlp_gain)
        gate_proj = jnp.dot(normed_mlp, w_gate, preferred_element_type=jnp.float32)
        up_proj = jnp.dot(normed_mlp, w_up, preferred_element_type=jnp.float32)
        hidden_chunks.append((jax.nn.silu(gate_proj) * up_proj).astype(jnp.bfloat16))
    hidden = jnp.concatenate(hidden_chunks, axis=0)
    after_all = jnp.concatenate(after_chunks, axis=0)
    after_mine = lax.dynamic_slice_in_dim(after_all, ts_index * tok_rows, tok_rows, 0)
    out_cols = w_down.shape[1] // COL_CHUNKS
    mlp_parts = []
    previous_part = None
    for col in range(COL_CHUNKS):
        down = jnp.dot(
            hidden,
            w_down[:, col * out_cols : (col + 1) * out_cols],
            preferred_element_type=jnp.float32,
        ).astype(jnp.bfloat16)
        if previous_part is not None:
            down = after(previous_part, down)
        part = lax.psum_scatter(down, "ts", scatter_dimension=0, tiled=True)
        previous_part = part
        mlp_parts.append(part)
    mlp_mine = jnp.concatenate(mlp_parts, axis=1).astype(jnp.float32)
    layer_rows = (after_mine.astype(jnp.float32) + mlp_mine).astype(jnp.bfloat16)
    return layer_rows.reshape(1, tok_rows, layer_rows.shape[1])


def solution(mesh):
    return jax.shard_map(
        shards,
        mesh=mesh,
        in_specs=(
            P("dp", None, "ts"),
            P("dp", None, "ts"),
            P("dp"),
            P("dp", None),
            P(),
            P(None, "ts"),
            P(None, "ts"),
            P(None, "ts"),
            P("ts", None),
            P(),
            P(None, "ts"),
            P(None, "ts"),
            P("ts", None),
        ),
        out_specs=P("dp", "ts", None),
        check_vma=False,
    )
```

profile of v0, /device:TPU:0, one launch (start us, length us, event | category | flops | bytes accessed | tf_op | source)
XLA Modules:
  0.0 565.7 jit_solution(9591049494155157957)
XLA Ops:
  7.8 1.9 fusion.95
  9.8 1.1 copy.107
  14.0 25.7 %all-gather.4.cloned.1.call-done = bf16[128,8320]{1,0:T(8,128)(2,1)} async-done(((bf16[16,8320]{1,0:T(8,128)(2,1)}), bf16[128,8320]{1,0:T(8,128)(2,1)}) %all-gather.4.cloned.1.call-update) | async-done | bytes 2129936 | tf_op jit(solution)/shard_map/all_gather | solution.py:102
  40.8 2.0 convolution_convert_fusion
  42.9 1.1 fusion.32
  44.9 57.9 %all-gather.6.cloned.1.call-done = bf16[512,4096]{1,0:T(8,128)(2,1)} async-done(((bf16[512,256]{1,0:T(8,128)(2,1)}), bf16[512,4096]{1,0:T(8,128)(2,1)}) %all-gather.6.cloned.1.call-update) | async-done | bytes 4194320 | tf_op jit(solution)/shard_map/all_gather | solution.py:141
  104.5 1.7 multiply_cosine_fusion
  106.3 1.3 fusion.25
  107.5 3.1 fusion.8
  110.6 1.7 fusion.10
  112.3 2.0 copy-done.6
  114.3 1.4 fusion.132
  115.9 1.0 fusion.88
  117.1 3.7 convolution_convert_fusion.7
  121.5 1.6 collective-permute-start
  123.1 3.8 fusion.133
  126.9 2.1 reshape_reshape.13
  129.0 1.7 fusion.116
  130.7 1.4 subtract_convert_fusion.1
  132.1 1.0 pad_maximum_fusion.4
  134.8 4.0 fusion.124
  138.8 2.0 convolution_convert_fusion.5
  140.8 3.2 convolution_convert_fusion.2
  144.1 17.8 %all-gather.8.cloned.1.call-done = bf16[512,4096]{1,0:T(8,128)(2,1)} async-done(((bf16[512,256]{1,0:T(8,128)(2,1)}), bf16[512,4096]{1,0:T(8,128)(2,1)}) %all-gather.8.cloned.1.call-update) | async-done | bytes 4194320 | tf_op jit(solution)/shard_map/all_gather | solution.py:141
  161.9 3.2 fusion.12
  165.3 1.7 fusion.14
  167.0 2.0 copy-done.4
  168.9 1.4 fusion.134
  171.0 4.4 convolution_convert_fusion.6
  177.1 3.7 fusion.135
  180.8 1.4 reshape_reshape.15
  183.5 1.3 collective-permute-done.1
  185.9 4.6 fusion.127
  190.5 2.7 fusion.41
  193.2 3.3 convolution_convert_fusion.1
  196.5 74.1 %all-reduce.4.cloned.1.call-done = bf16[512,4096]{1,0:T(8,128)(2,1)} async-done(((bf16[512,4096]{1,0:T(8,128)(2,1)}), bf16[512,4096]{1,0:T(8,128)(2,1)}) %all-reduce.4.cloned.1.call-update) | async-done | bytes 4194320 | tf_op jit(solution)/shard_map/psum | solution.py:181
  270.7 5.6 fusion.2
  276.3 7.5 %fusion.39 = f32[512,768]{1,0:T(8,128)S(1)} fusion(bf16[4096,768]{1,0:T(8,128)(2,1)} %param.27, bf16[512,4096]{1,0:T(8,128)(2,1)S(1)} %get-tuple-element.38, f32[4096]{0:T(1024)S(1)} %copy-done.27, f32[512]{0:T(512)S(1)} %add_rsqrt_fusion.1), kind=kOutput, calls=%fused_computation.59 | convolution fusion | flops 3229614080 | bytes 12077056 | tf_op jit(solution)/shard_map/dot_general | solution.py:188
  283.8 3.6 multiply_convert_fusion.1
  287.4 89.4 %all-reduce.6.cloned.1.call-done = bf16[512,4096]{1,0:T(8,128)(2,1)} async-done(((bf16[512,4096]{1,0:T(8,128)(2,1)}), bf16[512,4096]{1,0:T(8,128)(2,1)}) %all-reduce.6.cloned.1.call-update) | async-done | bytes 4194320 | tf_op jit(solution)/shard_map/psum | solution.py:181
  376.9 5.6 fusion.5
  382.5 7.2 %fusion.36 = f32[512,768]{1,0:T(8,128)S(1)} fusion(bf16[4096,768]{1,0:T(8,128)(2,1)} %param.27, bf16[512,4096]{1,0:T(8,128)(2,1)S(1)} %get-tuple-element.40, f32[512]{0:T(512)S(1)} %add_rsqrt_fusion, f32[4096]{0:T(1024)S(1)} %copy-done.27), kind=kOutput, calls=%fused_computation.58 | convolution fusion | flops 3229614080 | bytes 12077056 | tf_op jit(solution)/shard_map/dot_general | solution.py:188
  389.8 3.6 multiply_convert_fusion
  393.4 5.0 convolution_convert_fusion.4
  398.5 7.7 %convolution_convert_fusion.3 = bf16[1024,2048]{1,0:T(8,128)(2,1)} fusion(bf16[768,4096]{1,0:T(8,128)(2,1)} %param.29, bf16[512,768]{1,0:T(8,128)(2,1)S(1)} %multiply_convert_fusion, bf16[512,768]{1,0:T(8,128)(2,1)S(1)} %multiply_convert_fusion.1), kind=kOutput, calls=%fused_computation.34 | convolution fusion | flops 3226468352 | bytes 8912896 | tf_op jit(solution)/shard_map/dot_general | solution.py:198
  406.1 69.7 %reduce-scatter.3.cloned.1.call-done = bf16[64,2048]{1,0:T(8,128)(2,1)} async-done(((bf16[1024,2048]{1,0:T(8,128)(2,1)}), bf16[64,2048]{1,0:T(8,128)(2,1)}) %reduce-scatter.3.cloned.1.call-update) | async-done | bytes 262160 | tf_op jit(solution)/shard_map/reduce_scatter | solution.py:205
  475.9 80.6 %reduce-scatter.5.cloned.1.call-done = bf16[64,2048]{1,0:T(8,128)(2,1)} async-done(((bf16[1024,2048]{1,0:T(8,128)(2,1)}), bf16[64,2048]{1,0:T(8,128)(2,1)}) %reduce-scatter.5.cloned.1.call-update) | async-done | bytes 262160 | tf_op jit(solution)/shard_map/reduce_scatter | solution.py:205
  556.5 2.2 fusion.49
  (130 shorter events, 15.7 us)
Async XLA Ops:
  6.5 134.3 %copy-start = (bf16[256,4096]{1,0:T(8,128)(2,1)S(1)}, bf16[256,4096]{1,0:T(8,128)(2,1)}, u32[]{:S(2)}) copy-start(bf16[256,4096]{1,0:T(8,128)(2,1)} %param.25) | copy-start | bytes 6291460
  6.5 36.4 %copy-start.26 = (bf16[1,1024,256]{2,1,0:T(8,128)(2,1)S(1)}, bf16[1,1024,256]{2,1,0:T(8,128)(2,1)}, u32[]{:S(2)}) copy-start(bf16[1,1024,256]{2,1,0:T(8,128)(2,1)} %param.17) | copy-start | bytes 1572868
  6.5 33.2 %all-gather.4.cloned.1.call-start = ((), (), s32[]{:S(2)}) async-start(), calls=%async_computation.2 | async-start | bytes 2396160 | tf_op jit(solution)/shard_map/all_gather | solution.py:102
  10.9 92.6 %copy-start.16 = (s32[1,1024]{1,0:T(1,128)S(1)}, s32[1,1024]{1,0:T(1,128)}, u32[]{:S(2)}) copy-start(s32[1,1024]{1,0:T(1,128)} %param.20) | copy-start | bytes 12292
  11.7 91.2 %all-gather.6.cloned.1.call-start = ((), (), s32[]{:S(2)}) async-start(), calls=%async_computation.3 | async-start | bytes 4456448 | tf_op jit(solution)/shard_map/all_gather | solution.py:141
  44.0 66.6 %copy-start.17 = (f32[4096]{0:T(1024)S(1)}, f32[4096]{0:T(1024)}, u32[]{:S(2)}) copy-start(f32[4096]{0:T(1024)} %param.21) | copy-start | bytes 49156
  44.9 117.0 %all-gather.8.cloned.1.call-start = ((), (), s32[]{:S(2)}) async-start(), calls=%async_computation.5 | async-start | bytes 4456448 | tf_op jit(solution)/shard_map/all_gather | solution.py:141
  102.9 167.7 %all-reduce.4.cloned.1.call-start = ((), (), s32[]{:S(2)}) async-start(), calls=%async_computation.4 | async-start | bytes 8388608 | tf_op jit(solution)/shard_map/psum | solution.py:181
  102.9 7.7 %copy-start.3 = (bf16[512,4096]{1,0:T(8,128)(2,1)S(1)}, bf16[512,4096]{1,0:T(8,128)(2,1)}, u32[]{:S(2)}) copy-start(bf16[512,4096]{1,0:T(8,128)(2,1)} %all-gather.6.cloned.1.call-done) | copy-start | bytes 12582916
  103.6 7.0 %copy-start.22 = (f32[512]{0:T(512)}, f32[512]{0:T(512)S(1)}, u32[]{:S(2)}) copy-start(f32[512]{0:T(512)S(1)} %get-tuple-element.71) | copy-start | bytes 6148
  103.6 7.0 %copy-start.24 = (f32[512]{0:T(512)}, f32[512]{0:T(512)S(1)}, u32[]{:S(2)}) copy-start(f32[512]{0:T(512)S(1)} %get-tuple-element.72) | copy-start | bytes 6148
  110.6 3.7 copy-start.10
  112.3 2.0 copy-start.6
  114.3 2.7 copy-start.11
  117.1 6.0 %copy-start.7 = (bf16[512,4096]{1,0:T(8,128)(2,1)S(1)}, bf16[512,4096]{1,0:T(8,128)(2,1)}, u32[]{:S(2)}) copy-start(bf16[512,4096]{1,0:T(8,128)(2,1)} %copy-done.6) | copy-start | bytes 12582916
  121.5 9.2 %copy-start.14 = (f32[512,64]{0,1:T(8,128)S(1)}, f32[512,64]{0,1:T(8,128)}, u32[]{:S(2)}) copy-start(f32[512,64]{0,1:T(8,128)} %get-tuple-element.81) | copy-start | bytes 393220
  121.5 11.7 %collective-permute-start = (bf16[512,128]{0,1:T(8,128)(2,1)}, bf16[512,128]{0,1:T(8,128)(2,1)}, u32[]{:S(2)}, u32[]{:S(2)}) collective-permute-start(bf16[512,128]{0,1:T(8,128)(2,1)} %pad_maximum_fusion.6), channel_id=1, source_target_pairs={{0,1},{1,0},{2,3},{3,2},{4,5},{5,4},{6,7},{7,6},{8,9},{9,8},{10,11... | collective-permute-start | bytes 393224 | tf_op jit(solution)/shard_map/ppermute | solution.py:22
  134.8 4.0 copy-start.20
  134.8 4.0 copy-start.21
  144.0 232.8 %all-reduce.6.cloned.1.call-start = ((), (), s32[]{:S(2)}) async-start(), calls=%async_computation.6 | async-start | bytes 8388608 | tf_op jit(solution)/shard_map/psum | solution.py:181
  161.9 3.4 copy-start.2
  167.0 2.0 copy-start.4
  168.9 1.6 copy-start.23
  168.9 1.6 copy-start.25
  171.0 6.0 %copy-start.5 = (bf16[512,4096]{1,0:T(8,128)(2,1)S(1)}, bf16[512,4096]{1,0:T(8,128)(2,1)}, u32[]{:S(2)}) copy-start(bf16[512,4096]{1,0:T(8,128)(2,1)} %copy-done.4) | copy-start | bytes 12582916
  176.1 6.5 %copy-start.13 = (f32[512,64]{0,1:T(8,128)S(1)}, f32[512,64]{0,1:T(8,128)}, u32[]{:S(2)}) copy-start(f32[512,64]{0,1:T(8,128)} %get-tuple-element.78) | copy-start | bytes 393220
  176.1 8.7 %collective-permute-start.1 = (bf16[512,128]{0,1:T(8,128)(2,1)}, bf16[512,128]{0,1:T(8,128)(2,1)}, u32[]{:S(2)}, u32[]{:S(2)}) collective-permute-start(bf16[512,128]{0,1:T(8,128)(2,1)} %pad_maximum_fusion.7), channel_id=1, source_target_pairs={{0,1},{1,0},{2,3},{3,2},{4,5},{5,4},{6,7},{7,6},{8,9},{9,8},{10,11... | collective-permute-start | bytes 393224 | tf_op jit(solution)/shard_map/ppermute | solution.py:22
  180.8 5.1 copy-start.12
  185.8 4.6 copy-start.18
  185.9 4.6 copy-start.19
  270.6 5.7 %copy-start.27 = (f32[4096]{0:T(1024)S(1)}, f32[4096]{0:T(1024)}, u32[]{:S(2)}) copy-start(f32[4096]{0:T(1024)} %param.26) | copy-start | bytes 49156
  270.6 205.3 %reduce-scatter.3.cloned.1.call-start = ((), (), s32[]{:S(2)}) async-start(), calls=%async_computation.7 | async-start | bytes 4456448 | tf_op jit(solution)/shard_map/reduce_scatter | solution.py:205
  270.6 13.1 %slice-start = ((s8[6291456]{0:T(1024)(128)(4,1)}), s8[4194304]{0:T(1024)(128)(4,1)S(1)}, s32[]{:S(2)}) async-start(s8[6291456]{0:T(1024)(128)(4,1)} %bitcast.109), calls=%async_computation.9 | async-start | bytes 8388608
  276.2 7.5 %copy-start.8 = (bf16[512,4096]{1,0:T(8,128)(2,1)}, bf16[512,4096]{1,0:T(8,128)(2,1)S(1)}, u32[]{:S(2)}) copy-start(bf16[512,4096]{1,0:T(8,128)(2,1)S(1)} %get-tuple-element.38) | copy-start | bytes 12582916
  276.3 7.5 %slice-start.1 = ((s8[6291456]{0:T(1024)(128)(4,1)}), s8[2097152]{0:T(1024)(128)(4,1)S(1)}, s32[]{:S(2)}) async-start(s8[6291456]{0:T(1024)(128)(4,1)} %bitcast.109), calls=%async_computation.10 | async-start | bytes 4194304
  376.9 12.9 %slice-start.2 = ((s8[6291456]{0:T(1024)(128)(4,1)}), s8[4194304]{0:T(1024)(128)(4,1)S(1)}, s32[]{:S(2)}) async-start(s8[6291456]{0:T(1024)(128)(4,1)} %bitcast.111), calls=%async_computation.11 | async-start | bytes 8388608
  382.4 7.3 %copy-start.9 = (bf16[512,4096]{1,0:T(8,128)(2,1)}, bf16[512,4096]{1,0:T(8,128)(2,1)S(1)}, u32[]{:S(2)}) copy-start(bf16[512,4096]{1,0:T(8,128)(2,1)S(1)} %get-tuple-element.40) | copy-start | bytes 12582916
  382.5 7.2 %slice-start.3 = ((s8[6291456]{0:T(1024)(128)(4,1)}), s8[2097152]{0:T(1024)(128)(4,1)S(1)}, s32[]{:S(2)}) async-start(s8[6291456]{0:T(1024)(128)(4,1)} %bitcast.111), calls=%async_computation.12 | async-start | bytes 4194304
  382.5 10.9 %slice-start.4 = ((s8[6291456]{0:T(1024)(128)(4,1)}), s8[4194304]{0:T(1024)(128)(4,1)S(1)}, s32[]{:S(2)}) async-start(s8[6291456]{0:T(1024)(128)(4,1)} %bitcast.113), calls=%async_computation.13 | async-start | bytes 8388608
  389.7 3.6 slice-start.5
  398.4 158.1 %reduce-scatter.5.cloned.1.call-start = ((), (), s32[]{:S(2)}) async-start(), calls=%async_computation.8 | async-start | bytes 4456448 | tf_op jit(solution)/shard_map/reduce_scatter | solution.py:205
  475.9 80.6 %copy-start.15 = (bf16[64,2048]{1,0:T(8,128)(2,1)S(1)}, bf16[64,2048]{1,0:T(8,128)(2,1)}, u32[]{:S(2)}) copy-start(bf16[64,2048]{1,0:T(8,128)(2,1)} %reduce-scatter.3.cloned.1.call-done) | copy-start | bytes 786436
  475.9 82.8 %copy-start.1 = (bf16[256,4096]{1,0:T(8,128)(2,1)S(1)}, bf16[256,4096]{1,0:T(8,128)(2,1)}, u32[]{:S(2)}) copy-start(bf16[256,4096]{1,0:T(8,128)(2,1)} %param.25) | copy-start | bytes 6291460
Sparse Core Ops, SparseCore 0:
  11.8 27.8 all-gather.3
  45.0 57.8 all-gather.5
  105.0 56.8 all-gather.7
  165.1 105.4 all-reduce.3
  273.8 103.0 all-reduce.5
  398.5 77.2 reduce-scatter.2
  479.6 76.8 reduce-scatter.4
where the time goes:
time: 573 us; the launch traced here: 566 us
  waiting for transfers between devices  417 us (73%)
  matrix products  75.9 us (13%)
  other arithmetic  42.6 us (7%)
  between operations  14.4 us (3%)
  local copies, waits for them, and re-layouts  13.4 us (2%)
    psum x2, waiting for transfers between devices, shards(): attn_sum = lax.psum(partial_rows, 'ts')  164 us
    reduce_scatter x2, waiting for transfers between devices, shards(): part = lax.psum_scatter(down, 'ts', scatter_dimension=0, tiled=True)  150 us
    all_gather x2, waiting for transfers between devices, shards(): packed = lax.all_gather(local_rows, 'ts', axis=1, tiled=True)  75.7 us
    all_gather x1, waiting for transfers between devices, shards(): lax.all_gather(jnp.concatenate([flat_bridge, slot_cols], axis=1), 'dp', a...  25.7 us
    reduce_sum x4, other arithmetic, norm_rows(): jnp.mean(widened * widened, axis=-1, keepdims=True) + norm_epsilon  17.5 us
    dot_general x2, matrix products, shards(): gate_proj = jnp.dot(normed_mlp, w_gate, preferred_element_type=jnp.float32)  14.7 us
    dot_general x2, matrix products, shards(): jnp.dot(hidden, w_down[:, col * out_cols:(col + 1) * out_cols], preferred...  12.6 us
  transfers between devices with their start and end apart: 9, of which 8 were waited for; matrix products, arithmetic and copies ran while one was open for 17% of the time, Pallas kernels for 0%

commit v1 on v0

--- a/solution.py
+++ b/solution.py
@@ -10,6 +10,11 @@
 norm_epsilon = 1e-05
 rope_base = 500000.0
 masked_score = -1e30
+
+
+def add_all(shard, mesh_axis):
+    parts = lax.all_gather(shard, mesh_axis)
+    return jnp.sum(parts, axis=0)
 
 
 def partner_2(block, axis, apart):
@@ -178,7 +183,7 @@
         )
         if previous_sum is not None:
             partial_rows = after(previous_sum, partial_rows)
-        attn_sum = lax.psum(partial_rows, "ts")
+        attn_sum = add_all(partial_rows, "ts")
         previous_sum = attn_sum
         after_attn = (packed.astype(jnp.float32) + attn_sum.astype(jnp.float32)).astype(
             jnp.bfloat16

time: 573 us -> 1140 us (1.99)
  waiting for transfers between devices: 417 us -> 940 us
  other arithmetic: 42.6 us -> 90.2 us
    all_gather x0 -> x2, waiting for transfers between devices: none -> 687 us  [add_all(): parts = lax.all_gather(shard, mesh_axis)]
    psum x2 -> x0, waiting for transfers between devices: 164 us -> none  [shards(): attn_sum = lax.psum(partial_rows, 'ts')]
    reduce_sum x0 -> x2, other arithmetic: none -> 47.4 us  [add_all(): return jnp.sum(parts, axis=0)]
  transfers between devices with their start and end apart: 9 -> 9, of which waited for: 8 -> 8; matrix products, arithmetic and copies ran while one was open for 17% -> 8% of each run, Pallas kernels for 0% -> 0%
where the time goes in v1:
time: 1140 us
  waiting for transfers between devices  940 us (82%)
  other arithmetic  90.2 us (8%)
  matrix products  76.2 us (7%)
  between operations  14.4 us (1%)
  local copies, waits for them, and re-layouts  13.4 us (1%)
    all_gather x2, waiting for transfers between devices, add_all(): parts = lax.all_gather(shard, mesh_axis)  687 us
    reduce_scatter x2, waiting for transfers between devices, shards(): part = lax.psum_scatter(down, 'ts', scatter_dimension=0, tiled=True)  150 us
    all_gather x2, waiting for transfers between devices, shards(): packed = lax.all_gather(local_rows, 'ts', axis=1, tiled=True)  76.9 us
    reduce_sum x2, other arithmetic, add_all(): return jnp.sum(parts, axis=0)  47.4 us
    all_gather x1, waiting for transfers between devices, shards(): lax.all_gather(jnp.concatenate([flat_bridge, slot_cols], axis=1), 'dp', a...  25.7 us
  transfers between devices with their start and end apart: 9, of which 8 were waited for; matrix products, arithmetic and copies ran while one was open for 8% of the time, Pallas kernels for 0%

profile of v1, /device:TPU:0, one launch (start us, length us, event | category | flops | bytes accessed | tf_op | source)
XLA Modules:
  0.0 1137.0 jit_solution(1720552616174948454)
XLA Ops:
  7.9 1.9 fusion.95
  10.0 1.1 copy.107
  14.2 25.7 %all-gather.8.cloned.1.call-done = bf16[128,8320]{1,0:T(8,128)(2,1)} async-done(((bf16[16,8320]{1,0:T(8,128)(2,1)}), bf16[128,8320]{1,0:T(8,128)(2,1)}) %all-gather.8.cloned.1.call-update) | async-done | bytes 2129936 | tf_op jit(solution)/shard_map/all_gather | solution.py:107
  40.9 2.0 convolution_convert_fusion
  43.1 1.1 fusion.32
  45.1 57.9 %all-gather.10.cloned.1.call-done = bf16[512,4096]{1,0:T(8,128)(2,1)} async-done(((bf16[512,256]{1,0:T(8,128)(2,1)}), bf16[512,4096]{1,0:T(8,128)(2,1)}) %all-gather.10.cloned.1.call-update) | async-done | bytes 4194320 | tf_op jit(solution)/shard_map/all_gather | solution.py:146
  104.7 1.7 multiply_cosine_fusion
  106.4 3.1 fusion.8
  109.5 1.7 fusion.10
  111.2 1.9 copy-done.6
  113.1 1.4 fusion.132
  115.9 3.7 convolution_convert_fusion.7
  120.2 1.6 collective-permute-start
  121.9 3.7 fusion.133
  125.6 2.1 reshape_reshape.13
  127.7 1.7 fusion.116
  129.4 1.4 subtract_convert_fusion.1
  130.8 1.0 pad_maximum_fusion.4
  133.5 3.4 fusion.124
  136.9 2.1 convolution_convert_fusion.5
  139.0 3.3 convolution_convert_fusion.2
  142.4 1.3 fusion.25
  143.6 18.9 %all-gather.12.cloned.1.call-done = bf16[512,4096]{1,0:T(8,128)(2,1)} async-done(((bf16[512,256]{1,0:T(8,128)(2,1)}), bf16[512,4096]{1,0:T(8,128)(2,1)}) %all-gather.12.cloned.1.call-update) | async-done | bytes 4194320 | tf_op jit(solution)/shard_map/all_gather | solution.py:146
  162.5 3.2 fusion.12
  166.0 1.7 fusion.14
  167.7 2.0 copy-done.4
  169.6 1.4 fusion.134
  171.7 4.5 convolution_convert_fusion.6
  177.9 4.1 fusion.135
  182.0 1.5 reshape_reshape.15
  186.0 4.6 fusion.127
  190.7 2.7 fusion.41
  193.4 3.3 convolution_convert_fusion.1
  196.7 335.8 %all-gather.14.cloned.1.call-done = bf16[8192,4096]{1,0:T(8,128)(2,1)} async-done(((bf16[512,4096]{1,0:T(8,128)(2,1)}), bf16[8192,4096]{1,0:T(8,128)(2,1)}) %all-gather.14.cloned.1.call-update) | async-done | bytes 67108880 | tf_op jit(solution)/shard_map/all_gather | solution.py:16
  532.5 23.7 %reduce_sum.100 = bf16[512,4096]{1,0:T(8,128)(2,1)} reduce(bf16[16,512,4096]{2,1,0:T(8,128)(2,1)} %bitcast.11, bf16[]{:T(256)} %constant.137.clone.1), dimensions={0}, to_apply=%region_7.8 | reduce | flops 31457280 | bytes 71303168 | tf_op jit(solution)/shard_map/reduce_sum | solution.py:17
  556.3 5.6 fusion.2
  561.9 7.8 fusion.39
  569.7 3.6 multiply_convert_fusion.1
  573.4 351.2 %all-gather.16.cloned.1.call-done = bf16[8192,4096]{1,0:T(8,128)(2,1)} async-done(((bf16[512,4096]{1,0:T(8,128)(2,1)}), bf16[8192,4096]{1,0:T(8,128)(2,1)}) %all-gather.16.cloned.1.call-update) | async-done | bytes 67108880 | tf_op jit(solution)/shard_map/all_gather | solution.py:16
  924.6 23.7 %reduce_sum.103 = bf16[512,4096]{1,0:T(8,128)(2,1)} reduce(bf16[16,512,4096]{2,1,0:T(8,128)(2,1)} %bitcast.20, bf16[]{:T(256)} %constant.137.clone.1), dimensions={0}, to_apply=%region_11.12 | reduce | flops 31457280 | bytes 71303168 | tf_op jit(solution)/shard_map/reduce_sum | solution.py:17
  948.3 5.6 fusion.5
  953.9 7.2 fusion.36
  961.2 3.6 multiply_convert_fusion
  964.8 5.0 convolution_convert_fusion.4
  969.9 7.7 convolution_convert_fusion.3
  977.6 69.6 %reduce-scatter.3.cloned.1.call-done = bf16[64,2048]{1,0:T(8,128)(2,1)} async-done(((bf16[1024,2048]{1,0:T(8,128)(2,1)}), bf16[64,2048]{1,0:T(8,128)(2,1)}) %reduce-scatter.3.cloned.1.call-update) | async-done | bytes 262160 | tf_op jit(solution)/shard_map/reduce_scatter | solution.py:210
  1047.3 80.5 %reduce-scatter.5.cloned.1.call-done = bf16[64,2048]{1,0:T(8,128)(2,1)} async-done(((bf16[1024,2048]{1,0:T(8,128)(2,1)}), bf16[64,2048]{1,0:T(8,128)(2,1)}) %reduce-scatter.5.cloned.1.call-update) | async-done | bytes 262160 | tf_op jit(solution)/shard_map/reduce_scatter | solution.py:210
  1127.8 2.2 fusion.49
  (128 shorter events, 17.0 us)
Async XLA Ops:
  6.5 132.4 %copy-start = (bf16[256,4096]{1,0:T(8,128)(2,1)S(1)}, bf16[256,4096]{1,0:T(8,128)(2,1)}, u32[]{:S(2)}) copy-start(bf16[256,4096]{1,0:T(8,128)(2,1)} %param.25) | copy-start | bytes 6291460
  6.5 36.6 %copy-start.24 = (bf16[1,1024,256]{2,1,0:T(8,128)(2,1)S(1)}, bf16[1,1024,256]{2,1,0:T(8,128)(2,1)}, u32[]{:S(2)}) copy-start(bf16[1,1024,256]{2,1,0:T(8,128)(2,1)} %param.17) | copy-start | bytes 1572868
  6.5 33.4 %all-gather.8.cloned.1.call-start = ((), (), s32[]{:S(2)}) async-start(), calls=%async_computation.2 | async-start | bytes 2396160 | tf_op jit(solution)/shard_map/all_gather | solution.py:107
  11.1 92.6 %copy-start.16 = (s32[1,1024]{1,0:T(1,128)S(1)}, s32[1,1024]{1,0:T(1,128)}, u32[]{:S(2)}) copy-start(s32[1,1024]{1,0:T(1,128)} %param.20) | copy-start | bytes 12292
  11.8 91.2 %all-gather.10.cloned.1.call-start = ((), (), s32[]{:S(2)}) async-start(), calls=%async_computation.3 | async-start | bytes 4456448 | tf_op jit(solution)/shard_map/all_gather | solution.py:146
  43.1 66.4 %copy-start.17 = (f32[4096]{0:T(1024)S(1)}, f32[4096]{0:T(1024)}, u32[]{:S(2)}) copy-start(f32[4096]{0:T(1024)} %param.21) | copy-start | bytes 49156
  45.1 117.5 %all-gather.12.cloned.1.call-start = ((), (), s32[]{:S(2)}) async-start(), calls=%async_computation.4 | async-start | bytes 4456448 | tf_op jit(solution)/shard_map/all_gather | solution.py:146
  103.1 429.4 %all-gather.14.cloned.1.call-start = ((), (), s32[]{:S(2)}) async-start(), calls=%async_computation.7 | async-start | bytes 71303168 | tf_op jit(solution)/shard_map/all_gather | solution.py:16
  103.1 6.4 copy-start.3
  109.5 3.6 copy-start.10
  111.2 2.0 copy-start.6
  113.1 2.7 copy-start.11
  115.8 6.0 copy-start.7
  120.2 9.1 copy-start.14
  120.2 11.6 %collective-permute-start = (bf16[512,128]{0,1:T(8,128)(2,1)}, bf16[512,128]{0,1:T(8,128)(2,1)}, u32[]{:S(2)}, u32[]{:S(2)}) collective-permute-start(bf16[512,128]{0,1:T(8,128)(2,1)} %pad_maximum_fusion.6), channel_id=1, source_target_pairs={{0,1},{1,0},{2,3},{3,2},{4,5},{5,4},{6,7},{7,6},{8,9},{9,8},{10,11... | collective-permute-start | bytes 393224 | tf_op jit(solution)/shard_map/ppermute | solution.py:27
  133.5 3.4 copy-start.21
  133.5 3.4 copy-start.22
  142.3 23.5 %copy-start.18 = (f32[4096]{0:T(1024)S(1)}, f32[4096]{0:T(1024)}, u32[]{:S(2)}) copy-start(f32[4096]{0:T(1024)} %param.21) | copy-start | bytes 49156
  142.3 782.3 %all-gather.16.cloned.1.call-start = ((), (), s32[]{:S(2)}) async-start(), calls=%async_computation.8 | async-start | bytes 71303168 | tf_op jit(solution)/shard_map/all_gather | solution.py:16
  162.5 3.4 copy-start.2
  167.7 2.0 copy-start.4
  169.6 1.6 copy-start.23
  171.7 6.2 copy-start.5
  176.9 7.1 copy-start.13
  176.9 8.1 collective-permute-start.1
  182.0 4.0 copy-start.12
  186.0 4.7 copy-start.19
  186.0 4.6 copy-start.20
  556.2 5.7 copy-start.25
  556.2 491.0 %reduce-scatter.3.cloned.1.call-start = ((), (), s32[]{:S(2)}) async-start(), calls=%async_computation.5 | async-start | bytes 4456448 | tf_op jit(solution)/shard_map/reduce_scatter | solution.py:210
  556.3 13.5 %slice-start = ((s8[6291456]{0:T(1024)(128)(4,1)}), s8[4194304]{0:T(1024)(128)(4,1)S(1)}, s32[]{:S(2)}) async-start(s8[6291456]{0:T(1024)(128)(4,1)} %bitcast.111), calls=%async_computation.9 | async-start | bytes 8388608
  561.9 7.8 copy-start.8
  561.9 7.8 slice-start.1
  948.3 12.8 %slice-start.2 = ((s8[6291456]{0:T(1024)(128)(4,1)}), s8[4194304]{0:T(1024)(128)(4,1)S(1)}, s32[]{:S(2)}) async-start(s8[6291456]{0:T(1024)(128)(4,1)} %bitcast.113), calls=%async_computation.11 | async-start | bytes 8388608
  953.9 7.2 copy-start.9
  953.9 7.2 slice-start.3
  953.9 10.9 slice-start.4
  961.2 3.6 slice-start.5
  969.8 157.9 %reduce-scatter.5.cloned.1.call-start = ((), (), s32[]{:S(2)}) async-start(), calls=%async_computation.6 | async-start | bytes 4456448 | tf_op jit(solution)/shard_map/reduce_scatter | solution.py:210
  1047.2 80.6 %copy-start.15 = (bf16[64,2048]{1,0:T(8,128)(2,1)S(1)}, bf16[64,2048]{1,0:T(8,128)(2,1)}, u32[]{:S(2)}) copy-start(bf16[64,2048]{1,0:T(8,128)(2,1)} %reduce-scatter.3.cloned.1.call-done) | copy-start | bytes 786436
  1047.3 82.7 %copy-start.1 = (bf16[256,4096]{1,0:T(8,128)(2,1)S(1)}, bf16[256,4096]{1,0:T(8,128)(2,1)}, u32[]{:S(2)}) copy-start(bf16[256,4096]{1,0:T(8,128)(2,1)} %param.25) | copy-start | bytes 6291460
Sparse Core Ops, SparseCore 0:
  12.0 27.8 all-gather.7
  45.2 57.8 all-gather.9
  105.2 57.3 all-gather.11
  164.5 367.8 all-gather.13
  556.3 368.2 all-gather.15
  970.0 77.2 reduce-scatter.2
  1050.9 76.8 reduce-scatter.4
